TPU v7x, 128 devices: a whole 4x4x4 slice. The times are simulated.
128 devices in a mesh: req: 4 (over z), vocab: 32 (over y, x, core).
Axes of the slice: x: 4, y: 4, z: 4, core: 2. Of those that a mesh axis runs over, the one named last changes fastest.
Arguments:
- hidden: bfloat16 [16, 1536, 2048], P('req', 'vocab'), may hold values from -80 to 80
- norm_gain: float32 [2048], replicated, may hold values from 0.6 to 1.4
- head_weight: bfloat16 [2048, 32000], P(None, 'vocab'), may hold values from -2 to 2
- token_ids: int32 [16, 1536], P('req', 'vocab'), may hold values from 0 to 31999
- lengths: int32 [16], replicated, may hold values from 1 to 1536, 15360 in all
- group_ids: int32 [16], replicated, may hold values from 0 to 3
Outputs:
- logprob: float32 [16, 1536], P('req', 'vocab')
- entropy: float32 [16, 1536], P('req', 'vocab')
- centered: float32 [16], replicated
Inputs may be any that keep to these rules, and one draw needn't show every extreme that they name: The lengths sum to 15360; the longest is 1536.
All inputs are finite; a program needn't handle non-finite values.
Results may differ from a plain program's by a relative error of at most 0.00093.
Values may be sent and summed in bfloat16 or wider, within the bound.
No kernel may reach another device: no remote copies, remote signals or barrier semaphores. Data moves between devices by JAX's collectives and lax.ppermute only.
A program may use at most 128 MiB of HBM per device.

v0:
```python
import jax
import jax.numpy as jnp
from jax import lax
from jax.sharding import PartitionSpec as P

norm_eps = 1e-06


def slice_stats(rows, tokens, weight, offset):
    row_count = rows.shape[0]
    block_len = min(512, row_count)
    columns = jnp.arange(weight.shape[1], dtype=jnp.int32)
    results = []
    for block_start in range(0, row_count, block_len):
        block_rows = rows[block_start : block_start + block_len]
        local_ids = tokens[block_start : block_start + block_len] - offset
        logits = jnp.dot(block_rows, weight, preferred_element_type=jnp.float32)
        row_top = jnp.max(logits, axis=1)
        exps = jnp.exp(logits - row_top[:, None])
        exp_total = jnp.sum(exps, axis=1)
        moment = jnp.sum(exps * logits, axis=1)
        picked = jnp.sum(jnp.where(columns[None, :] == local_ids[:, None], logits, 0.0), axis=1)
        results.append((row_top, exp_total, moment, picked))
    return tuple((jnp.concatenate([item[slot] for item in results]) for slot in range(4)))


def body(hidden, norm_gain, head_weight, token_ids, lengths, group_ids):
    req_dev, pos_dev, model_width = hidden.shape
    vocab_dev = head_weight.shape[1]
    vocab_index = lax.axis_index("vocab")
    req_index = lax.axis_index("req")
    values = hidden.astype(jnp.float32)
    squares = jnp.mean(values * values, axis=-1, keepdims=True)
    normed = (values * lax.rsqrt(squares + norm_eps) * norm_gain).astype(jnp.bfloat16)
    own_rows = req_dev * pos_dev
    flat_rows = normed.reshape(own_rows, model_width)
    flat_tokens = token_ids.reshape(own_rows)
    offset = vocab_index * vocab_dev
    fresh = slice_stats(
        lax.all_gather(flat_rows, "vocab", axis=0, tiled=True),
        lax.all_gather(flat_tokens, "vocab", axis=0, tiled=True),
        head_weight,
        offset,
    )
    maxima, sums, moments, picked = tuple((new_part for new_part in fresh))
    own_start = vocab_index * own_rows
    row_top = lax.pmax(maxima, "vocab")
    rescale = jnp.exp(maxima - row_top)
    exp_total, moment, token_logit = lax.psum((sums * rescale, moments * rescale, picked), "vocab")
    row_top = lax.dynamic_slice_in_dim(row_top, own_start, own_rows)
    exp_total = lax.dynamic_slice_in_dim(exp_total, own_start, own_rows)
    moment = lax.dynamic_slice_in_dim(moment, own_start, own_rows)
    token_logit = lax.dynamic_slice_in_dim(token_logit, own_start, own_rows)
    log_total = row_top + jnp.log(exp_total)
    raw_logprob = (token_logit - log_total).reshape(req_dev, pos_dev)
    raw_entropy = (log_total - moment / exp_total).reshape(req_dev, pos_dev)
    positions = vocab_index * pos_dev + jnp.arange(pos_dev, dtype=jnp.int32)
    own_lengths = lax.dynamic_slice_in_dim(lengths, req_index * req_dev, req_dev)
    is_live = positions[None, :] < own_lengths[:, None]
    logprob = jnp.where(is_live, raw_logprob, 0.0)
    entropy = jnp.where(is_live, raw_entropy, 0.0)
    partial_sums = jnp.sum(logprob, axis=1)
    request_count = lengths.shape[0]
    global_rows = req_index * req_dev + jnp.arange(req_dev, dtype=jnp.int32)
    slots = jnp.arange(request_count, dtype=jnp.int32)
    placed = jnp.sum(
        jnp.where(slots[None, :] == global_rows[:, None], partial_sums[:, None], 0.0), axis=0
    )
    seq_sum = lax.psum(placed, ("req", "vocab"))
    same = (group_ids[:, None] == group_ids[None, :]).astype(jnp.float32)
    members = jnp.sum(same, axis=1)
    group_mean = jnp.sum(same * seq_sum[None, :], axis=1) / members
    spread = jnp.sum(same * (seq_sum[None, :] - group_mean[:, None]) ** 2, axis=1) / members
    group_std = jnp.maximum(jnp.sqrt(spread), 1.0)
    centered = (seq_sum - group_mean) / group_std
    return (logprob, entropy, centered)


def solution(mesh):
    return jax.shard_map(
        body,
        mesh=mesh,
        in_specs=(P("req", "vocab", None), P(), P(None, "vocab"), P("req", "vocab"), P(), P()),
        out_specs=(P("req", "vocab"), P("req", "vocab"), P()),
        check_vma=False,
    )
```

profile of v0, /device:TPU:1, one launch (start us, length us, event | category | flops | bytes accessed | tf_op | source)
XLA Modules:
  0.0 505.1 jit_solution(15608291727772157882)
XLA Ops:
  7.2 1.4 fusion.36
  8.6 2.3 fusion.38
  11.2 0.6 dynamic-slice
  12.7 127.5 %all-reduce = s32[6144]{0:T(1024)S(1)} all-reduce(s32[6144]{0:T(1024)S(1)} %dynamic-update-slice), channel_id=1, replica_groups=mesh['req'=4,'vocab'=32] {'vocab'}, use_global_device_ids=true, to_apply=%add | all-reduce | flops 6144 | bytes 49152
  140.2 6.6 %fusion.45 = (f32[512]{0:T(512)S(1)}, f32[512,1000]{0,1:T(8,128)}) fusion(bf16[2048,1000]{0,1:T(8,128)(2,1)} %param.8, bf16[6144,2048]{1,0:T(8,128)(2,1)} %all-gather.2.cloned.1.call-done), kind=kOutput, calls=%fused_computation.170 | convolution fusion | flops 2097663488 | bytes 8243200 | tf_op jit(solution)/shard_map/dot_general | solution.py:17
  146.9 4.1 copy-done.12
  150.9 5.9 %fusion.46 = (f32[512]{0:T(512)S(1)}, f32[512,1000]{0,1:T(8,128)}) fusion(bf16[2048,1000]{0,1:T(8,128)(2,1)} %param.8, bf16[6144,2048]{1,0:T(8,128)(2,1)S(1)} %copy-done.12), kind=kOutput, calls=%fused_computation.171 | convolution fusion | flops 2097663488 | bytes 8243200 | tf_op jit(solution)/shard_map/dot_general | solution.py:17
  156.9 3.6 fusion.47
  160.5 3.6 fusion.48
  164.1 3.7 fusion.49
  167.8 3.6 fusion.50
  171.5 3.8 fusion.51
  175.3 3.6 fusion.52
  178.9 3.6 fusion.53
  182.6 3.6 fusion.54
  186.2 2.3 fusion.55
  188.5 3.6 fusion.56
  192.1 124.0 %pmax.7 = f32[6144]{0:T(1024)S(1)} all-reduce(f32[6144]{0:T(1024)S(1)} %constant_dynamic-update-slice_fusion.1), channel_id=1, replica_groups=mesh['req'=4,'vocab'=32] {'vocab'}, use_global_device_ids=true, to_apply=%region_26.27 | all-reduce | flops 6144 | bytes 49152 | tf_op jit(solution)/shard_map/pmax | solution.py:47
  316.1 3.7 multiply_reduce_fusion.10
  319.8 1.3 multiply_reduce_fusion.8
  321.4 0.6 copy-done.6
  322.0 1.3 multiply_reduce_fusion.6
  323.6 0.6 copy-done.4
  324.2 1.3 multiply_reduce_fusion.4
  325.8 0.6 copy-done.2
  326.4 1.3 multiply_reduce_fusion.2
  328.0 1.3 multiply_reduce_fusion
  329.6 0.6 fusion.39
  330.4 100.8 %all-reduce.4.cloned.1.call-done = (f32[6144]{0:T(1024)}, f32[6144]{0:T(1024)}, f32[6144]{0:T(1024)}) async-done(((f32[6144]{0:T(1024)}, f32[6144]{0:T(1024)}, f32[6144]{0:T(1024)}), (f32[6144]{0:T(1024)}, f32[6144]{0:T(1024)}, f32[6144]{0:T(1024)})) %all-reduce.4.cloned.1.call-update) | async-done | bytes 73744 | tf_op jit(solution)/shard_map/psum | solution.py:49
  431.3 0.8 divide_subtract_fusion
  432.2 0.8 fusion.44
  433.1 64.2 %psum.31 = f32[16]{0:T(128)S(1)} all-reduce(f32[16]{0:T(128)S(1)} %select_reduce_fusion.12), channel_id=1, replica_groups=mesh['req'=4,'vocab'=32] {'req','vocab'}, use_global_device_ids=true, to_apply=%region_55.56 | all-reduce | flops 16 | bytes 128 | tf_op jit(solution)/shard_map/psum | solution.py:69
  (100 shorter events, 3.0 us)
Async XLA Ops:
  7.2 4.0 copy-start.15
  7.2 3.9 copy-start.11
  7.2 133.0 %all-gather.2.cloned.1.call-start = ((), (), s32[]{:S(2)}) async-start(), calls=%async_computation | async-start | bytes 25952256 | tf_op jit(solution)/shard_map/all_gather | solution.py:40
  11.0 420.3 %all-reduce.4.cloned.1.call-start = ((), (), s32[]{:S(2)}) async-start(), calls=%async_computation.1 | async-start | bytes 147456 | tf_op jit(solution)/shard_map/psum | solution.py:49
  140.2 10.7 %copy-start.12 = (bf16[6144,2048]{1,0:T(8,128)(2,1)S(1)}, bf16[6144,2048]{1,0:T(8,128)(2,1)}, u32[]{:S(2)}) copy-start(bf16[6144,2048]{1,0:T(8,128)(2,1)} %all-gather.2.cloned.1.call-done) | copy-start | bytes 75497472
  150.9 5.9 %copy-start.13 = (bf16[2048,1000]{0,1:T(8,128)(2,1)S(1)}, bf16[2048,1000]{0,1:T(8,128)(2,1)}, u32[]{:S(2)}) copy-start(bf16[2048,1000]{0,1:T(8,128)(2,1)} %param.8) | copy-start | bytes 12288004
  316.1 3.7 copy-start.7
  316.1 3.7 copy-start.8
  319.8 1.6 copy-start.5
  319.8 2.2 copy-start.6
  322.0 1.6 copy-start.3
  322.0 2.2 copy-start.4
  324.2 1.6 copy-start.1
  324.2 2.2 copy-start.2
  326.4 1.6 copy-start
  328.0 2.4 copy-start.14
  328.0 169.3 %copy-start.10 = (s32[16]{0:T(128)S(1)}, s32[16]{0:T(128)}, u32[]{:S(2)}) copy-start(s32[16]{0:T(128)} %param.11) | copy-start | bytes 196
  329.6 0.6 copy-start.9
Sparse Core Ops, SparseCore 0:
  11.1 95.8 all-gather.1
  330.4 100.7 all-reduce.3
where the time goes:
time: 505 us
  blocking collectives  316 us (63%)
  waiting for transfers between devices  101 us (20%)
  matrix products  47.7 us (9%)
  other arithmetic  17.3 us (3%)
  between operations  15.1 us (3%)
  local copies, waits for them, and re-layouts  8.28 us (2%)
    unnamed x1, blocking collectives  127 us
    pmax x1, blocking collectives, body(): row_top = lax.pmax(maxima, 'vocab')  124 us
    psum x1, waiting for transfers between devices, body(): lax.psum((sums * rescale, moments * rescale, picked), 'vocab')  101 us
    psum x1, blocking collectives, body(): seq_sum = lax.psum(placed, ('req', 'vocab'))  64.2 us
    dot_general x12, matrix products, slice_stats(): logits = jnp.dot(block_rows, weight, preferred_element_type=jnp.float32)  47.7 us
    reduce_sum x6, other arithmetic, slice_stats(): moment = jnp.sum(exps * logits, axis=1)  10.3 us
  transfers between devices with their start and end apart: 2, of which 1 were waited for; matrix products, arithmetic and copies ran while one was open for 0% of the time, Pallas kernels for 0%

commit v1 on v0

--- a/solution.py
+++ b/solution.py
@@ -66,7 +66,7 @@
     placed = jnp.sum(
         jnp.where(slots[None, :] == global_rows[:, None], partial_sums[:, None], 0.0), axis=0
     )
-    seq_sum = lax.psum(placed, ("req", "vocab"))
+    seq_sum = jnp.sum(lax.all_gather(placed, ("req", "vocab")), axis=0)
     same = (group_ids[:, None] == group_ids[None, :]).astype(jnp.float32)
     members = jnp.sum(same, axis=1)
     group_mean = jnp.sum(same * seq_sum[None, :], axis=1) / members

time: 505 us -> 506 us (level)
    psum x1 -> x0, blocking collectives: 64.2 us -> none  [body(): seq_sum = lax.psum(placed, ('req', 'vocab'))]
    unnamed x1 -> x2, blocking collectives: 127 us -> 192 us
where the time goes in v1:
time: 506 us; the launch traced here: 505 us
  blocking collectives  316 us (62%)
  waiting for transfers between devices  101 us (20%)
  matrix products  47.7 us (9%)
  other arithmetic  17.3 us (3%)
  between operations  15.2 us (3%)
  local copies, waits for them, and re-layouts  8.63 us (2%)
    unnamed x2, blocking collectives  192 us
    pmax x1, blocking collectives, body(): row_top = lax.pmax(maxima, 'vocab')  124 us
    psum x1, waiting for transfers between devices, body(): lax.psum((sums * rescale, moments * rescale, picked), 'vocab')  101 us
    dot_general x12, matrix products, slice_stats(): logits = jnp.dot(block_rows, weight, preferred_element_type=jnp.float32)  47.7 us
    reduce_sum x6, other arithmetic, slice_stats(): moment = jnp.sum(exps * logits, axis=1)  10.3 us
  transfers between devices with their start and end apart: 2, of which 1 were waited for; matrix products, arithmetic and copies ran while one was open for 0% of the time, Pallas kernels for 0%

profile of v1, /device:TPU:1, one launch (start us, length us, event | category | flops | bytes accessed | tf_op | source)
XLA Modules:
  0.0 505.5 jit_solution(15452840009662678816)
XLA Ops:
  7.2 1.4 fusion.36
  8.6 2.3 fusion.38
  11.2 0.6 dynamic-slice
  12.7 127.5 %all-reduce = s32[6144]{0:T(1024)S(1)} all-reduce(s32[6144]{0:T(1024)S(1)} %dynamic-update-slice), channel_id=1, replica_groups=mesh['req'=4,'vocab'=32] {'vocab'}, use_global_device_ids=true, to_apply=%add | all-reduce | flops 6144 | bytes 49152
  140.2 6.6 %fusion.45 = (f32[512]{0:T(512)S(1)}, f32[512,1000]{0,1:T(8,128)}) fusion(bf16[2048,1000]{0,1:T(8,128)(2,1)} %param.8, bf16[6144,2048]{1,0:T(8,128)(2,1)} %all-gather.3.cloned.1.call-done), kind=kOutput, calls=%fused_computation.170 | convolution fusion | flops 2097663488 | bytes 8243200 | tf_op jit(solution)/shard_map/dot_general | solution.py:17
  146.9 4.1 copy-done.12
  150.9 5.9 %fusion.46 = (f32[512]{0:T(512)S(1)}, f32[512,1000]{0,1:T(8,128)}) fusion(bf16[2048,1000]{0,1:T(8,128)(2,1)} %param.8, bf16[6144,2048]{1,0:T(8,128)(2,1)S(1)} %copy-done.12), kind=kOutput, calls=%fused_computation.171 | convolution fusion | flops 2097663488 | bytes 8243200 | tf_op jit(solution)/shard_map/dot_general | solution.py:17
  156.9 3.6 fusion.47
  160.5 3.6 fusion.48
  164.1 3.7 fusion.49
  167.8 3.6 fusion.50
  171.5 3.8 fusion.51
  175.3 3.6 fusion.52
  178.9 3.6 fusion.53
  182.6 3.6 fusion.54
  186.2 2.3 fusion.55
  188.5 3.6 fusion.56
  192.1 124.0 %pmax.7 = f32[6144]{0:T(1024)S(1)} all-reduce(f32[6144]{0:T(1024)S(1)} %constant_dynamic-update-slice_fusion.1), channel_id=1, replica_groups=mesh['req'=4,'vocab'=32] {'vocab'}, use_global_device_ids=true, to_apply=%region_26.27 | all-reduce | flops 6144 | bytes 49152 | tf_op jit(solution)/shard_map/pmax | solution.py:47
  316.1 3.7 multiply_reduce_fusion.10
  319.8 1.3 multiply_reduce_fusion.8
  321.4 0.6 copy-done.6
  322.0 1.3 multiply_reduce_fusion.6
  323.6 0.6 copy-done.4
  324.2 1.3 multiply_reduce_fusion.4
  325.8 0.6 copy-done.2
  326.4 1.3 multiply_reduce_fusion.2
  328.0 1.3 multiply_reduce_fusion
  329.6 0.6 fusion.39
  330.4 100.8 %all-reduce.5.cloned.1.call-done = (f32[6144]{0:T(1024)}, f32[6144]{0:T(1024)}, f32[6144]{0:T(1024)}) async-done(((f32[6144]{0:T(1024)}, f32[6144]{0:T(1024)}, f32[6144]{0:T(1024)}), (f32[6144]{0:T(1024)}, f32[6144]{0:T(1024)}, f32[6144]{0:T(1024)})) %all-reduce.5.cloned.1.call-update) | async-done | bytes 73744 | tf_op jit(solution)/shard_map/psum | solution.py:49
  431.3 0.8 divide_subtract_fusion
  432.2 0.8 fusion.44
  433.4 64.2 %all-reduce.1 = f32[2048]{0:T(1024)S(1)} all-reduce(f32[2048]{0:T(1024)S(1)} %dynamic-update-slice.1), channel_id=2, replica_groups=mesh['req'=4,'vocab'=32] {'req','vocab'}, use_global_device_ids=true, to_apply=%add.1 | all-reduce | flops 2048 | bytes 16384
  (104 shorter events, 3.3 us)
Async XLA Ops:
  7.2 4.0 copy-start.15
  7.2 3.9 copy-start.11
  7.2 133.0 %all-gather.3.cloned.1.call-start = ((), (), s32[]{:S(2)}) async-start(), calls=%async_computation | async-start | bytes 25952256 | tf_op jit(solution)/shard_map/all_gather | solution.py:40
  11.0 420.3 %all-reduce.5.cloned.1.call-start = ((), (), s32[]{:S(2)}) async-start(), calls=%async_computation.1 | async-start | bytes 147456 | tf_op jit(solution)/shard_map/psum | solution.py:49
  140.2 10.7 %copy-start.12 = (bf16[6144,2048]{1,0:T(8,128)(2,1)S(1)}, bf16[6144,2048]{1,0:T(8,128)(2,1)}, u32[]{:S(2)}) copy-start(bf16[6144,2048]{1,0:T(8,128)(2,1)} %all-gather.3.cloned.1.call-done) | copy-start | bytes 75497472
  150.9 5.9 %copy-start.13 = (bf16[2048,1000]{0,1:T(8,128)(2,1)S(1)}, bf16[2048,1000]{0,1:T(8,128)(2,1)}, u32[]{:S(2)}) copy-start(bf16[2048,1000]{0,1:T(8,128)(2,1)} %param.8) | copy-start | bytes 12288004
  316.1 3.7 copy-start.7
  316.1 3.7 copy-start.8
  319.8 1.6 copy-start.5
  319.8 2.2 copy-start.6
  322.0 1.6 copy-start.3
  322.0 2.2 copy-start.4
  324.2 1.6 copy-start.1
  324.2 2.2 copy-start.2
  326.4 1.6 copy-start
  328.0 2.4 copy-start.14
  328.0 169.7 %copy-start.10 = (s32[16]{0:T(128)S(1)}, s32[16]{0:T(128)}, u32[]{:S(2)}) copy-start(s32[16]{0:T(128)} %param.11) | copy-start | bytes 196
  329.6 0.6 copy-start.9
Sparse Core Ops, SparseCore 0:
  11.1 95.8 all-gather.2
  330.4 100.7 all-reduce.4
